TPU v7x, 256 devices: a whole 4x4x8 slice. The times are simulated.
256 devices in a mesh: dp: 32 (over x, y, core), shard: 8 (over z).
Axes of the slice: x: 4, y: 4, z: 8, core: 2. Of those that a mesh axis runs over, the one named last changes fastest.
Arguments:
- audio: bfloat16 [65536, 512], P(('dp', 'shard')), may hold values from -6 to 6
- cotangent: bfloat16 [65536, 512], P(('dp', 'shard')), may hold values from -6 to 6
- clip_lengths: int32 [256, 8], P(('dp', 'shard')), may hold values from 1 to 128, 256 in all within a row
- conv_weight: bfloat16 [3584, 512], P('shard'), may hold values from -0.09375 to 0.09375
- mix_weight: bfloat16 [512, 512], P('shard'), may hold values from -0.25 to 0.25
- conv_bias: float32 [512], replicated, may hold values from -3 to 3
- alpha_in: float32 [512], replicated, may hold values from 0.5 to 3
- alpha_mid: float32 [512], replicated, may hold values from 0.5 to 3
Outputs:
- in_grad: bfloat16 [65536, 512], P(('dp', 'shard'))
- conv_grad: float32 [3584, 512], P(('dp', 'shard'))
- mix_grad: float32 [512, 512], P(('dp', 'shard'))
- vector_grad: float32 [4, 512], P(None, ('dp', 'shard'))
Inputs may be any that keep to these rules, and one draw needn't show every extreme that they name: `clip_lengths`: each device's clip lengths sum to 256; the largest on each device is 128.
All inputs are finite; a program needn't handle non-finite values.
Results may differ from a plain program's by a relative error of at most 0.01.
Values may be sent and summed in bfloat16 or wider, within the bound.
No kernel may reach another device: no remote copies, remote signals or barrier semaphores. Data moves between devices by JAX's collectives and lax.ppermute only.
A program may use at most 64 MiB of HBM per device.

v0:
```python
import jax
import jax.numpy as jnp
from jax import lax
from jax.sharding import PartitionSpec as P

C = 512
TAPS = 7
DILATION_SIZE = 9


def shift_rows(block, tap_offset, fill):
    rows = block.shape[0]
    shift_amount = min(abs(tap_offset), rows)
    if shift_amount == 0:
        return block
    edge_padding = jnp.full((shift_amount,) + block.shape[1:], fill, block.dtype)
    if tap_offset > 0:
        return jnp.concatenate([block[shift_amount:], edge_padding], axis=0)
    return jnp.concatenate([edge_padding, block[: rows - shift_amount]], axis=0)


def clip_masks(lengths_row, rows):
    clip_ends = jnp.cumsum(lengths_row)
    position = jnp.arange(rows, dtype=jnp.int32)
    clip_id = jnp.sum((position[:, None] >= clip_ends[None, :]).astype(jnp.int32), axis=1)
    result = []
    for kernel_tap_index in range(TAPS):
        tap_offset = (kernel_tap_index - 3) * DILATION_SIZE
        result.append(shift_rows(clip_id, tap_offset, -1) == clip_id)
    return result


def snake_parts(value, alpha):
    sine = jnp.sin(alpha * value)
    double = jnp.sin(2.0 * alpha * value)
    return (
        value + sine * sine / alpha,
        1.0 + double,
        value * double / alpha - sine * sine / (alpha * alpha),
    )


def per_device(
    audio, cotangent, clip_lengths, conv_weight, mix_weight, conv_bias, alpha_in, alpha_mid
):
    rows = audio.shape[0]
    same_clip_flags = clip_masks(clip_lengths[0], rows)
    mix_full = lax.all_gather(mix_weight, "shard", axis=0, tiled=True)
    audio_f = audio.astype(jnp.float32)
    act_in, slope_in, dalpha_in = snake_parts(audio_f, alpha_in)
    first = act_in.astype(jnp.bfloat16)
    columns = []
    for kernel_tap_index in range(TAPS):
        tap_offset = (kernel_tap_index - 3) * DILATION_SIZE
        moved = shift_rows(first, tap_offset, 0)
        columns.append(
            jnp.where(same_clip_flags[kernel_tap_index][:, None], moved, jnp.zeros_like(moved))
        )
    unfolded = jnp.concatenate(columns, axis=1)
    product = jnp.dot(
        unfolded,
        lax.all_gather(conv_weight, "shard", axis=0, tiled=True),
        preferred_element_type=jnp.float32,
    )
    pre = product + conv_bias
    act_mid, slope_mid, dalpha_mid = snake_parts(pre, alpha_mid)
    second = act_mid.astype(jnp.bfloat16)
    mix_term = lax.dot_general(
        second, cotangent, (((0,), (0,)), ((), ())), preferred_element_type=jnp.float32
    )
    second_gradient = lax.dot_general(
        cotangent, mix_full, (((1,), (1,)), ((), ())), preferred_element_type=jnp.float32
    )
    d_pre = (second_gradient * slope_mid).astype(jnp.bfloat16)
    convolution_part = lax.dot_general(
        unfolded, d_pre, (((0,), (0,)), ((), ())), preferred_element_type=jnp.float32
    )
    d_unf = lax.dot_general(
        d_pre,
        lax.all_gather(conv_weight, "shard", axis=0, tiled=True),
        (((1,), (1,)), ((), ())),
        preferred_element_type=jnp.float32,
    ).astype(jnp.bfloat16)
    d_first = jnp.zeros((rows, C), jnp.float32)
    for kernel_tap_index in range(TAPS):
        tap_offset = (kernel_tap_index - 3) * DILATION_SIZE
        piece = d_unf[:, kernel_tap_index * C : (kernel_tap_index + 1) * C].astype(jnp.float32)
        piece = jnp.where(same_clip_flags[kernel_tap_index][:, None], piece, jnp.zeros_like(piece))
        d_first = d_first + shift_rows(piece, -tap_offset, 0.0)
    in_grad = (cotangent.astype(jnp.float32) + d_first * slope_in).astype(jnp.bfloat16)
    vectors = jnp.stack(
        [
            jnp.sum(d_pre.astype(jnp.float32), axis=0),
            jnp.sum(cotangent.astype(jnp.float32), axis=0),
            jnp.sum(d_first * dalpha_in, axis=0),
            jnp.sum(second_gradient * dalpha_mid, axis=0),
        ]
    )
    conv_grad, mix_grad, vector_grad = (
        lax.psum_scatter(convolution_part, ("dp", "shard"), scatter_dimension=0, tiled=True),
        lax.psum_scatter(mix_term, ("dp", "shard"), scatter_dimension=0, tiled=True),
        lax.psum_scatter(vectors, ("dp", "shard"), scatter_dimension=1, tiled=True),
    )
    return (in_grad, conv_grad, mix_grad, vector_grad)


def solution(mesh):
    placed = (
        P(("dp", "shard"), None),
        P(("dp", "shard"), None),
        P(("dp", "shard"), None),
        P("shard", None),
        P("shard", None),
        P(),
        P(),
        P(),
    )
    return jax.shard_map(
        per_device,
        mesh=mesh,
        in_specs=placed,
        out_specs=(
            P(("dp", "shard"), None),
            P(("dp", "shard"), None),
            P(("dp", "shard"), None),
            P(None, ("dp", "shard")),
        ),
        check_vma=False,
    )
```

profile of v0, /device:TPU:2, one launch (start us, length us, event | category | flops | bytes accessed | tf_op | source)
XLA Modules:
  0.0 1037.1 jit_solution(11425878607155914596)
XLA Ops:
  10.8 30.8 %all_gather.7 = bf16[512,512]{1,0:T(8,128)(2,1)S(1)} all-gather(bf16[64,512]{1,0:T(8,128)(2,1)} %param.12), channel_id=1, replica_groups=mesh['dp'=32,'shard'=8] {'shard'}, dimensions={0}, use_global_device_ids=true | all-gather | bytes 589824 | tf_op jit(solution)/shard_map/all_gather | solution.py:48
  47.6 17.5 %all-gather.2.cloned.1.call-done = bf16[3584,512]{1,0:T(8,128)(2,1)} async-done(((bf16[448,512]{1,0:T(8,128)(2,1)}), bf16[3584,512]{1,0:T(8,128)(2,1)}) %all-gather.2.cloned.1.call-update) | async-done | bytes 3670032 | tf_op jit(solution)/shard_map/all_gather | solution.py:62
  72.0 4.9 convert_reduce_fusion.1
  77.0 4.1 fusion.23
  81.0 597.1 %fusion = f32[16,512]{1,0:T(8,128)S(1)} fusion(f32[3584,512]{1,0:T(8,128)} %fusion.23), kind=kCustom, calls=%all-reduce-scatter | all-reduce-scatter fusion | flops 2097153 | bytes 7372800
  689.2 4.0 collective-permute-start.31
  693.7 4.0 collective-permute-done.31
  697.7 51.7 %collective-permute-start.26 = (f32[16,512]{1,0:T(8,128)S(1)}, f32[16,512]{1,0:T(8,128)S(1)}, u32[]{:S(2)}, u32[]{:S(2)}) collective-permute-start(f32[16,512]{1,0:T(8,128)S(1)} %fusion), channel_id=1, source_target_pairs={{0,27},{1,28},{2,29},{3,30},{4,31},{5,32},{6,33},{7,34},{8,35},{9,... | collective-permute-start | bytes 98312
  753.4 43.3 %collective-permute-start.23 = (f32[16,512]{1,0:T(8,128)S(1)}, f32[16,512]{1,0:T(8,128)S(1)}, u32[]{:S(2)}, u32[]{:S(2)}) collective-permute-start(f32[16,512]{1,0:T(8,128)S(1)} %fusion), channel_id=1, source_target_pairs={{0,24},{1,25},{2,26},{3,27},{4,28},{5,29},{6,30},{7,31},{8,32},{9,... | collective-permute-start | bytes 98312
  796.7 3.6 collective-permute-start.22
  805.1 5.1 collective-permute-start.19
  810.2 3.7 collective-permute-start.18
  820.7 3.9 fusion.13
  829.7 4.2 collective-permute-start.12
  833.9 5.1 collective-permute-start.11
  843.7 3.4 collective-permute-start.9
  851.1 4.4 collective-permute-start.6
  857.5 80.1 %all-reduce.20 = f32[4,512]{1,0:T(4,128)S(1)} all-reduce(f32[4,512]{1,0:T(4,128)S(1)} %pad_maximum_fusion), channel_id=4, replica_groups=mesh['dp'=32,'shard'=8] {'dp','shard'}, use_global_device_ids=true, to_apply=%region_8.9.clone | all-reduce | flops 2048 | bytes 16384
  937.6 4.4 collective-permute-start.4
  942.1 4.5 collective-permute-start.3
  949.0 3.3 collective-permute-start.1
  952.3 4.2 collective-permute-start
  962.4 3.8 concatenate.76
  966.9 62.1 %all-reduce.24.cloned.1.call-done = f32[512,512]{1,0:T(8,128)} async-done(((f32[512,512]{1,0:T(8,128)}), f32[512,512]{1,0:T(8,128)}) %all-reduce.24.cloned.1.call-update) | async-done | bytes 1048592
  (103 shorter events, 69.1 us)
Async XLA Ops:
  7.2 57.9 %all-gather.2.cloned.1.call-start = ((), (), s32[]{:S(2)}) async-start(), calls=%async_computation | async-start | bytes 4128768 | tf_op jit(solution)/shard_map/all_gather | solution.py:62
  7.9 1021.1 %all-reduce.24.cloned.1.call-start = ((), (), s32[]{:S(2)}) async-start(), calls=%async_computation.1 | async-start | bytes 2097152
  678.2 71.2 %collective-permute-start.30 = (f32[16,512]{1,0:T(8,128)S(1)}, f32[16,512]{1,0:T(8,128)S(1)}, u32[]{:S(2)}, u32[]{:S(2)}) collective-permute-start(f32[16,512]{1,0:T(8,128)S(1)} %fusion), channel_id=1, source_target_pairs={{0,31},{1,32},{2,33},{3,34},{4,35},{5,36},{6,37},{7,38},{8,39},{9,... | collective-permute-start | bytes 98312
  680.1 71.3 %collective-permute-start.29 = (f32[16,512]{1,0:T(8,128)S(1)}, f32[16,512]{1,0:T(8,128)S(1)}, u32[]{:S(2)}, u32[]{:S(2)}) collective-permute-start(f32[16,512]{1,0:T(8,128)S(1)} %fusion), channel_id=1, source_target_pairs={{0,30},{1,31},{2,32},{3,33},{4,34},{5,35},{6,36},{7,37},{8,38},{9,... | collective-permute-start | bytes 98312
  682.0 71.4 %collective-permute-start.28 = (f32[16,512]{1,0:T(8,128)S(1)}, f32[16,512]{1,0:T(8,128)S(1)}, u32[]{:S(2)}, u32[]{:S(2)}) collective-permute-start(f32[16,512]{1,0:T(8,128)S(1)} %fusion), channel_id=1, source_target_pairs={{0,29},{1,30},{2,31},{3,32},{4,33},{5,34},{6,35},{7,36},{8,37},{9,... | collective-permute-start | bytes 98312
  684.0 112.7 %collective-permute-start.27 = (f32[16,512]{1,0:T(8,128)S(1)}, f32[16,512]{1,0:T(8,128)S(1)}, u32[]{:S(2)}, u32[]{:S(2)}) collective-permute-start(f32[16,512]{1,0:T(8,128)S(1)} %fusion), channel_id=1, source_target_pairs={{0,28},{1,29},{2,30},{3,31},{4,32},{5,33},{6,34},{7,35},{8,36},{9,... | collective-permute-start | bytes 98312
  697.7 102.6 %collective-permute-start.26 = (f32[16,512]{1,0:T(8,128)S(1)}, f32[16,512]{1,0:T(8,128)S(1)}, u32[]{:S(2)}, u32[]{:S(2)}) collective-permute-start(f32[16,512]{1,0:T(8,128)S(1)} %fusion), channel_id=1, source_target_pairs={{0,27},{1,28},{2,29},{3,30},{4,31},{5,32},{6,33},{7,34},{8,35},{9,... | collective-permute-start | bytes 98312
  749.4 52.9 %collective-permute-start.25 = (f32[16,512]{1,0:T(8,128)S(1)}, f32[16,512]{1,0:T(8,128)S(1)}, u32[]{:S(2)}, u32[]{:S(2)}) collective-permute-start(f32[16,512]{1,0:T(8,128)S(1)} %fusion), channel_id=1, source_target_pairs={{0,26},{1,27},{2,28},{3,29},{4,30},{5,31},{6,32},{7,33},{8,34},{9,... | collective-permute-start | bytes 98312
  751.5 53.6 %collective-permute-start.24 = (f32[16,512]{1,0:T(8,128)S(1)}, f32[16,512]{1,0:T(8,128)S(1)}, u32[]{:S(2)}, u32[]{:S(2)}) collective-permute-start(f32[16,512]{1,0:T(8,128)S(1)} %fusion), channel_id=1, source_target_pairs={{0,25},{1,26},{2,27},{3,28},{4,29},{5,30},{6,31},{7,32},{8,33},{9,... | collective-permute-start | bytes 98312
  753.4 56.8 %collective-permute-start.23 = (f32[16,512]{1,0:T(8,128)S(1)}, f32[16,512]{1,0:T(8,128)S(1)}, u32[]{:S(2)}, u32[]{:S(2)}) collective-permute-start(f32[16,512]{1,0:T(8,128)S(1)} %fusion), channel_id=1, source_target_pairs={{0,24},{1,25},{2,26},{3,27},{4,28},{5,29},{6,30},{7,31},{8,32},{9,... | collective-permute-start | bytes 98312
  796.7 17.2 %collective-permute-start.22 = (f32[16,512]{1,0:T(8,128)S(1)}, f32[16,512]{1,0:T(8,128)S(1)}, u32[]{:S(2)}, u32[]{:S(2)}) collective-permute-start(f32[16,512]{1,0:T(8,128)S(1)} %fusion), channel_id=1, source_target_pairs={{0,23},{1,24},{2,25},{3,26},{4,27},{5,28},{6,29},{7,30},{8,31},{9,... | collective-permute-start | bytes 98312
  805.1 19.5 %collective-permute-start.19 = (f32[16,512]{1,0:T(8,128)S(1)}, f32[16,512]{1,0:T(8,128)S(1)}, u32[]{:S(2)}, u32[]{:S(2)}) collective-permute-start(f32[16,512]{1,0:T(8,128)S(1)} %fusion), channel_id=1, source_target_pairs={{0,20},{1,21},{2,22},{3,23},{4,24},{5,25},{6,26},{7,27},{8,28},{9,... | collective-permute-start | bytes 98312
  810.2 17.4 %collective-permute-start.18 = (f32[16,512]{1,0:T(8,128)S(1)}, f32[16,512]{1,0:T(8,128)S(1)}, u32[]{:S(2)}, u32[]{:S(2)}) collective-permute-start(f32[16,512]{1,0:T(8,128)S(1)} %fusion), channel_id=1, source_target_pairs={{0,19},{1,20},{2,21},{3,22},{4,23},{5,24},{6,25},{7,26},{8,27},{9,... | collective-permute-start | bytes 98312
  815.9 18.0 %collective-permute-start.16 = (f32[16,512]{1,0:T(8,128)S(1)}, f32[16,512]{1,0:T(8,128)S(1)}, u32[]{:S(2)}, u32[]{:S(2)}) collective-permute-start(f32[16,512]{1,0:T(8,128)S(1)} %fusion), channel_id=1, source_target_pairs={{0,17},{1,18},{2,19},{3,20},{4,21},{5,22},{6,23},{7,24},{8,25},{9,... | collective-permute-start | bytes 98312
  817.8 21.2 %collective-permute-start.15 = (f32[16,512]{1,0:T(8,128)S(1)}, f32[16,512]{1,0:T(8,128)S(1)}, u32[]{:S(2)}, u32[]{:S(2)}) collective-permute-start(f32[16,512]{1,0:T(8,128)S(1)} %fusion), channel_id=1, source_target_pairs={{0,16},{1,17},{2,18},{3,19},{4,20},{5,21},{6,22},{7,23},{8,24},{9,... | collective-permute-start | bytes 98312
  824.6 19.1 %collective-permute-start.14 = (f32[16,512]{1,0:T(8,128)S(1)}, f32[16,512]{1,0:T(8,128)S(1)}, u32[]{:S(2)}, u32[]{:S(2)}) collective-permute-start(f32[16,512]{1,0:T(8,128)S(1)} %fusion), channel_id=1, source_target_pairs={{0,15},{1,16},{2,17},{3,18},{4,19},{5,20},{6,21},{7,22},{8,23},{9,... | collective-permute-start | bytes 98312
  827.7 19.4 %collective-permute-start.13 = (f32[16,512]{1,0:T(8,128)S(1)}, f32[16,512]{1,0:T(8,128)S(1)}, u32[]{:S(2)}, u32[]{:S(2)}) collective-permute-start(f32[16,512]{1,0:T(8,128)S(1)} %fusion), channel_id=1, source_target_pairs={{0,14},{1,15},{2,16},{3,17},{4,18},{5,19},{6,20},{7,21},{8,22},{9,... | collective-permute-start | bytes 98312
  829.7 19.4 %collective-permute-start.12 = (f32[16,512]{1,0:T(8,128)S(1)}, f32[16,512]{1,0:T(8,128)S(1)}, u32[]{:S(2)}, u32[]{:S(2)}) collective-permute-start(f32[16,512]{1,0:T(8,128)S(1)} %fusion), channel_id=1, source_target_pairs={{0,13},{1,14},{2,15},{3,16},{4,17},{5,18},{6,19},{7,20},{8,21},{9,... | collective-permute-start | bytes 98312
  843.7 93.9 %collective-permute-start.9 = (f32[16,512]{1,0:T(8,128)S(1)}, f32[16,512]{1,0:T(8,128)S(1)}, u32[]{:S(2)}, u32[]{:S(2)}) collective-permute-start(f32[16,512]{1,0:T(8,128)S(1)} %fusion), channel_id=1, source_target_pairs={{0,10},{1,11},{2,12},{3,13},{4,14},{5,15},{6,16},{7,17},{8,18},{9,... | collective-permute-start | bytes 98312
  847.1 95.0 %collective-permute-start.8 = (f32[16,512]{1,0:T(8,128)S(1)}, f32[16,512]{1,0:T(8,128)S(1)}, u32[]{:S(2)}, u32[]{:S(2)}) collective-permute-start(f32[16,512]{1,0:T(8,128)S(1)} %fusion), channel_id=1, source_target_pairs={{0,9},{1,10},{2,11},{3,12},{4,13},{5,14},{6,15},{7,16},{8,17},{9,1... | collective-permute-start | bytes 98312
  849.1 97.5 %collective-permute-start.7 = (f32[16,512]{1,0:T(8,128)S(1)}, f32[16,512]{1,0:T(8,128)S(1)}, u32[]{:S(2)}, u32[]{:S(2)}) collective-permute-start(f32[16,512]{1,0:T(8,128)S(1)} %fusion), channel_id=1, source_target_pairs={{0,8},{1,9},{2,10},{3,11},{4,12},{5,13},{6,14},{7,15},{8,16},{9,17... | collective-permute-start | bytes 98312
  851.1 97.9 %collective-permute-start.6 = (f32[16,512]{1,0:T(8,128)S(1)}, f32[16,512]{1,0:T(8,128)S(1)}, u32[]{:S(2)}, u32[]{:S(2)}) collective-permute-start(f32[16,512]{1,0:T(8,128)S(1)} %fusion), channel_id=1, source_target_pairs={{0,7},{1,8},{2,9},{3,10},{4,11},{5,12},{6,13},{7,14},{8,15},{9,16}... | collective-permute-start | bytes 98312
  855.5 96.8 %collective-permute-start.5 = (f32[16,512]{1,0:T(8,128)S(1)}, f32[16,512]{1,0:T(8,128)S(1)}, u32[]{:S(2)}, u32[]{:S(2)}) collective-permute-start(f32[16,512]{1,0:T(8,128)S(1)} %fusion), channel_id=1, source_target_pairs={{0,6},{1,7},{2,8},{3,9},{4,10},{5,11},{6,12},{7,13},{8,14},{9,15},... | collective-permute-start | bytes 98312
  937.6 19.6 %collective-permute-start.4 = (f32[16,512]{1,0:T(8,128)S(1)}, f32[16,512]{1,0:T(8,128)S(1)}, u32[]{:S(2)}, u32[]{:S(2)}) collective-permute-start(f32[16,512]{1,0:T(8,128)S(1)} %fusion), channel_id=1, source_target_pairs={{0,5},{1,6},{2,7},{3,8},{4,9},{5,10},{6,11},{7,12},{8,13},{9,14},{... | collective-permute-start | bytes 98312
  (16 other events, 202.3 us)
Sparse Core Ops, SparseCore 0:
  9.8 55.2 all-gather.1
  686.0 342.8 all-reduce.23
where the time goes:
time: 1040 us
  blocking collectives  708 us (68%)
  starting transfers between devices  183 us (18%)
  waiting for transfers between devices  89.5 us (9%)
  matrix products  18.4 us (2%)
  between operations  14.7 us (1%)
  other arithmetic  14.6 us (1%)
    unnamed x2, blocking collectives  677 us
    unnamed x33, starting transfers between devices  183 us
    unnamed x35, waiting for transfers between devices  72.1 us
    all_gather x1, blocking collectives, per_device(): mix_full = lax.all_gather(mix_weight, 'shard', axis=0, tiled=True)  30.8 us
  transfers between devices with their start and end apart: 34, of which 6 were waited for; matrix products, arithmetic and copies ran while one was open for 2% of the time, Pallas kernels for 0%

commit v1 on v0

--- a/solution.py
+++ b/solution.py
@@ -45,7 +45,9 @@
 ):
     rows = audio.shape[0]
     same_clip_flags = clip_masks(clip_lengths[0], rows)
-    mix_full = lax.all_gather(mix_weight, "shard", axis=0, tiled=True)
+    mix_full = jnp.concatenate(
+        lax.all_to_all(jnp.stack([mix_weight] * lax.axis_size("shard")), "shard", 0, 0), axis=0
+    )
     audio_f = audio.astype(jnp.float32)
     act_in, slope_in, dalpha_in = snake_parts(audio_f, alpha_in)
     first = act_in.astype(jnp.bfloat16)

time: 1040 us -> 1040 us (level)
  blocking collectives: 708 us -> 678 us
  waiting for transfers between devices: 89.5 us -> 118 us
    all_gather x1 -> x0, blocking collectives: 30.8 us -> none  [per_device(): mix_full = lax.all_gather(mix_weight, 'shard', axis=0, tiled=True)]
    all_gather x1, waiting for transfers between devices: 17.5 us -> 44.3 us  [per_device(): lax.all_gather(conv_weight, 'shard', axis=0, tiled=True)]
  transfers between devices with their start and end apart: 34 -> 35, of which waited for: 6 -> 6; matrix products, arithmetic and copies ran while one was open for 2% -> 3% of each run, Pallas kernels for 0% -> 0%
where the time goes in v1:
time: 1040 us
  blocking collectives  678 us (65%)
  starting transfers between devices  190 us (18%)
  waiting for transfers between devices  118 us (11%)
  matrix products  18.4 us (2%)
  between operations  14.8 us (1%)
  other arithmetic  11.7 us (1%)
    unnamed x2, blocking collectives  678 us
    unnamed x33, starting transfers between devices  181 us
    unnamed x35, waiting for transfers between devices  73.4 us
    all_gather x1, waiting for transfers between devices, per_device(): lax.all_gather(conv_weight, 'shard', axis=0, tiled=True)  44.3 us
  transfers between devices with their start and end apart: 35, of which 6 were waited for; matrix products, arithmetic and copies ran while one was open for 3% of the time, Pallas kernels for 0%

profile of v1, /device:TPU:2, one launch (start us, length us, event | category | flops | bytes accessed | tf_op | source)
XLA Modules:
  0.0 1040.4 jit_solution(2561881116739494562)
XLA Ops:
  9.6 8.5 all-to-all-start
  23.6 44.3 %all-gather.2.cloned.1.call-done = bf16[3584,512]{1,0:T(8,128)(2,1)} async-done(((bf16[448,512]{1,0:T(8,128)(2,1)}), bf16[3584,512]{1,0:T(8,128)(2,1)}) %all-gather.2.cloned.1.call-update) | async-done | bytes 3670032 | tf_op jit(solution)/shard_map/all_gather | solution.py:64
  74.8 4.9 convert_reduce_fusion.1
  79.8 4.1 fusion.23
  83.8 598.2 %fusion = f32[16,512]{1,0:T(8,128)S(1)} fusion(f32[3584,512]{1,0:T(8,128)} %fusion.23), kind=kCustom, calls=%all-reduce-scatter | all-reduce-scatter fusion | flops 2097153 | bytes 7372800
  689.8 3.3 convolution_convert_fusion
  696.4 5.4 collective-permute-done.31
  701.9 50.8 %collective-permute-start.26 = (f32[16,512]{1,0:T(8,128)S(1)}, f32[16,512]{1,0:T(8,128)S(1)}, u32[]{:S(2)}, u32[]{:S(2)}) collective-permute-start(f32[16,512]{1,0:T(8,128)S(1)} %fusion), channel_id=1, source_target_pairs={{0,27},{1,28},{2,29},{3,30},{4,31},{5,32},{6,33},{7,34},{8,35},{9,... | collective-permute-start | bytes 98312
  756.7 43.3 %collective-permute-start.23 = (f32[16,512]{1,0:T(8,128)S(1)}, f32[16,512]{1,0:T(8,128)S(1)}, u32[]{:S(2)}, u32[]{:S(2)}) collective-permute-start(f32[16,512]{1,0:T(8,128)S(1)} %fusion), channel_id=1, source_target_pairs={{0,24},{1,25},{2,26},{3,27},{4,28},{5,29},{6,30},{7,31},{8,32},{9,... | collective-permute-start | bytes 98312
  800.0 3.4 collective-permute-start.22
  808.4 5.1 collective-permute-start.19
  813.6 3.7 collective-permute-start.18
  824.0 3.9 fusion.13
  833.0 4.2 collective-permute-start.12
  837.3 5.1 collective-permute-start.11
  847.0 3.4 collective-permute-start.9
  854.4 4.4 collective-permute-start.6
  860.9 80.1 %all-reduce.20 = f32[4,512]{1,0:T(4,128)S(1)} all-reduce(f32[4,512]{1,0:T(4,128)S(1)} %pad_maximum_fusion), channel_id=4, replica_groups=mesh['dp'=32,'shard'=8] {'dp','shard'}, use_global_device_ids=true, to_apply=%region_8.9.clone | all-reduce | flops 2048 | bytes 16384
  940.9 4.5 collective-permute-start.4
  945.4 4.5 collective-permute-start.3
  952.3 3.3 collective-permute-start.1
  955.6 4.2 collective-permute-start
  965.7 3.8 concatenate.76
  970.2 62.1 %all-reduce.24.cloned.1.call-done = f32[512,512]{1,0:T(8,128)} async-done(((f32[512,512]{1,0:T(8,128)}), f32[512,512]{1,0:T(8,128)}) %all-reduce.24.cloned.1.call-update) | async-done | bytes 1048592
  (107 shorter events, 67.3 us)
Async XLA Ops:
  7.2 60.7 %all-gather.2.cloned.1.call-start = ((), (), s32[]{:S(2)}) async-start(), calls=%async_computation.1 | async-start | bytes 4128768 | tf_op jit(solution)/shard_map/all_gather | solution.py:64
  9.6 65.2 %all-to-all-start = ((bf16[8,64,512]{2,1,0:T(8,128)(2,1)}), bf16[8,64,512]{2,1,0:T(8,128)(2,1)S(1)}, u32[]{:S(2)}, u32[]{:S(2)}) async-start(bf16[8,64,512]{2,1,0:T(8,128)(2,1)} %stack.12), calls=%async_computation | async-start | bytes 1048576 | tf_op jit(solution)/shard_map/all_to_all | solution.py:49
  18.1 1014.2 %all-reduce.24.cloned.1.call-start = ((), (), s32[]{:S(2)}) async-start(), calls=%async_computation.2 | async-start | bytes 2097152
  682.0 70.7 %collective-permute-start.30 = (f32[16,512]{1,0:T(8,128)S(1)}, f32[16,512]{1,0:T(8,128)S(1)}, u32[]{:S(2)}, u32[]{:S(2)}) collective-permute-start(f32[16,512]{1,0:T(8,128)S(1)} %fusion), channel_id=1, source_target_pairs={{0,31},{1,32},{2,33},{3,34},{4,35},{5,36},{6,37},{7,38},{8,39},{9,... | collective-permute-start | bytes 98312
  684.0 70.8 %collective-permute-start.29 = (f32[16,512]{1,0:T(8,128)S(1)}, f32[16,512]{1,0:T(8,128)S(1)}, u32[]{:S(2)}, u32[]{:S(2)}) collective-permute-start(f32[16,512]{1,0:T(8,128)S(1)} %fusion), channel_id=1, source_target_pairs={{0,30},{1,31},{2,32},{3,33},{4,34},{5,35},{6,36},{7,37},{8,38},{9,... | collective-permute-start | bytes 98312
  685.9 70.8 %collective-permute-start.28 = (f32[16,512]{1,0:T(8,128)S(1)}, f32[16,512]{1,0:T(8,128)S(1)}, u32[]{:S(2)}, u32[]{:S(2)}) collective-permute-start(f32[16,512]{1,0:T(8,128)S(1)} %fusion), channel_id=1, source_target_pairs={{0,29},{1,30},{2,31},{3,32},{4,33},{5,34},{6,35},{7,36},{8,37},{9,... | collective-permute-start | bytes 98312
  687.8 112.2 %collective-permute-start.27 = (f32[16,512]{1,0:T(8,128)S(1)}, f32[16,512]{1,0:T(8,128)S(1)}, u32[]{:S(2)}, u32[]{:S(2)}) collective-permute-start(f32[16,512]{1,0:T(8,128)S(1)} %fusion), channel_id=1, source_target_pairs={{0,28},{1,29},{2,30},{3,31},{4,32},{5,33},{6,34},{7,35},{8,36},{9,... | collective-permute-start | bytes 98312
  701.9 101.6 %collective-permute-start.26 = (f32[16,512]{1,0:T(8,128)S(1)}, f32[16,512]{1,0:T(8,128)S(1)}, u32[]{:S(2)}, u32[]{:S(2)}) collective-permute-start(f32[16,512]{1,0:T(8,128)S(1)} %fusion), channel_id=1, source_target_pairs={{0,27},{1,28},{2,29},{3,30},{4,31},{5,32},{6,33},{7,34},{8,35},{9,... | collective-permute-start | bytes 98312
  752.7 52.8 %collective-permute-start.25 = (f32[16,512]{1,0:T(8,128)S(1)}, f32[16,512]{1,0:T(8,128)S(1)}, u32[]{:S(2)}, u32[]{:S(2)}) collective-permute-start(f32[16,512]{1,0:T(8,128)S(1)} %fusion), channel_id=1, source_target_pairs={{0,26},{1,27},{2,28},{3,29},{4,30},{5,31},{6,32},{7,33},{8,34},{9,... | collective-permute-start | bytes 98312
  754.8 53.7 %collective-permute-start.24 = (f32[16,512]{1,0:T(8,128)S(1)}, f32[16,512]{1,0:T(8,128)S(1)}, u32[]{:S(2)}, u32[]{:S(2)}) collective-permute-start(f32[16,512]{1,0:T(8,128)S(1)} %fusion), channel_id=1, source_target_pairs={{0,25},{1,26},{2,27},{3,28},{4,29},{5,30},{6,31},{7,32},{8,33},{9,... | collective-permute-start | bytes 98312
  756.7 56.9 %collective-permute-start.23 = (f32[16,512]{1,0:T(8,128)S(1)}, f32[16,512]{1,0:T(8,128)S(1)}, u32[]{:S(2)}, u32[]{:S(2)}) collective-permute-start(f32[16,512]{1,0:T(8,128)S(1)} %fusion), channel_id=1, source_target_pairs={{0,24},{1,25},{2,26},{3,27},{4,28},{5,29},{6,30},{7,31},{8,32},{9,... | collective-permute-start | bytes 98312
  808.4 19.5 %collective-permute-start.19 = (f32[16,512]{1,0:T(8,128)S(1)}, f32[16,512]{1,0:T(8,128)S(1)}, u32[]{:S(2)}, u32[]{:S(2)}) collective-permute-start(f32[16,512]{1,0:T(8,128)S(1)} %fusion), channel_id=1, source_target_pairs={{0,20},{1,21},{2,22},{3,23},{4,24},{5,25},{6,26},{7,27},{8,28},{9,... | collective-permute-start | bytes 98312
  813.6 17.5 %collective-permute-start.18 = (f32[16,512]{1,0:T(8,128)S(1)}, f32[16,512]{1,0:T(8,128)S(1)}, u32[]{:S(2)}, u32[]{:S(2)}) collective-permute-start(f32[16,512]{1,0:T(8,128)S(1)} %fusion), channel_id=1, source_target_pairs={{0,19},{1,20},{2,21},{3,22},{4,23},{5,24},{6,25},{7,26},{8,27},{9,... | collective-permute-start | bytes 98312
  819.2 18.0 %collective-permute-start.16 = (f32[16,512]{1,0:T(8,128)S(1)}, f32[16,512]{1,0:T(8,128)S(1)}, u32[]{:S(2)}, u32[]{:S(2)}) collective-permute-start(f32[16,512]{1,0:T(8,128)S(1)} %fusion), channel_id=1, source_target_pairs={{0,17},{1,18},{2,19},{3,20},{4,21},{5,22},{6,23},{7,24},{8,25},{9,... | collective-permute-start | bytes 98312
  821.2 21.2 %collective-permute-start.15 = (f32[16,512]{1,0:T(8,128)S(1)}, f32[16,512]{1,0:T(8,128)S(1)}, u32[]{:S(2)}, u32[]{:S(2)}) collective-permute-start(f32[16,512]{1,0:T(8,128)S(1)} %fusion), channel_id=1, source_target_pairs={{0,16},{1,17},{2,18},{3,19},{4,20},{5,21},{6,22},{7,23},{8,24},{9,... | collective-permute-start | bytes 98312
  827.9 19.1 %collective-permute-start.14 = (f32[16,512]{1,0:T(8,128)S(1)}, f32[16,512]{1,0:T(8,128)S(1)}, u32[]{:S(2)}, u32[]{:S(2)}) collective-permute-start(f32[16,512]{1,0:T(8,128)S(1)} %fusion), channel_id=1, source_target_pairs={{0,15},{1,16},{2,17},{3,18},{4,19},{5,20},{6,21},{7,22},{8,23},{9,... | collective-permute-start | bytes 98312
  831.1 19.3 %collective-permute-start.13 = (f32[16,512]{1,0:T(8,128)S(1)}, f32[16,512]{1,0:T(8,128)S(1)}, u32[]{:S(2)}, u32[]{:S(2)}) collective-permute-start(f32[16,512]{1,0:T(8,128)S(1)} %fusion), channel_id=1, source_target_pairs={{0,14},{1,15},{2,16},{3,17},{4,18},{5,19},{6,20},{7,21},{8,22},{9,... | collective-permute-start | bytes 98312
  833.0 19.4 %collective-permute-start.12 = (f32[16,512]{1,0:T(8,128)S(1)}, f32[16,512]{1,0:T(8,128)S(1)}, u32[]{:S(2)}, u32[]{:S(2)}) collective-permute-start(f32[16,512]{1,0:T(8,128)S(1)} %fusion), channel_id=1, source_target_pairs={{0,13},{1,14},{2,15},{3,16},{4,17},{5,18},{6,19},{7,20},{8,21},{9,... | collective-permute-start | bytes 98312
  847.0 93.9 %collective-permute-start.9 = (f32[16,512]{1,0:T(8,128)S(1)}, f32[16,512]{1,0:T(8,128)S(1)}, u32[]{:S(2)}, u32[]{:S(2)}) collective-permute-start(f32[16,512]{1,0:T(8,128)S(1)} %fusion), channel_id=1, source_target_pairs={{0,10},{1,11},{2,12},{3,13},{4,14},{5,15},{6,16},{7,17},{8,18},{9,... | collective-permute-start | bytes 98312
  850.4 95.0 %collective-permute-start.8 = (f32[16,512]{1,0:T(8,128)S(1)}, f32[16,512]{1,0:T(8,128)S(1)}, u32[]{:S(2)}, u32[]{:S(2)}) collective-permute-start(f32[16,512]{1,0:T(8,128)S(1)} %fusion), channel_id=1, source_target_pairs={{0,9},{1,10},{2,11},{3,12},{4,13},{5,14},{6,15},{7,16},{8,17},{9,1... | collective-permute-start | bytes 98312
  852.4 97.5 %collective-permute-start.7 = (f32[16,512]{1,0:T(8,128)S(1)}, f32[16,512]{1,0:T(8,128)S(1)}, u32[]{:S(2)}, u32[]{:S(2)}) collective-permute-start(f32[16,512]{1,0:T(8,128)S(1)} %fusion), channel_id=1, source_target_pairs={{0,8},{1,9},{2,10},{3,11},{4,12},{5,13},{6,14},{7,15},{8,16},{9,17... | collective-permute-start | bytes 98312
  854.4 97.9 %collective-permute-start.6 = (f32[16,512]{1,0:T(8,128)S(1)}, f32[16,512]{1,0:T(8,128)S(1)}, u32[]{:S(2)}, u32[]{:S(2)}) collective-permute-start(f32[16,512]{1,0:T(8,128)S(1)} %fusion), channel_id=1, source_target_pairs={{0,7},{1,8},{2,9},{3,10},{4,11},{5,12},{6,13},{7,14},{8,15},{9,16}... | collective-permute-start | bytes 98312
  858.8 96.8 %collective-permute-start.5 = (f32[16,512]{1,0:T(8,128)S(1)}, f32[16,512]{1,0:T(8,128)S(1)}, u32[]{:S(2)}, u32[]{:S(2)}) collective-permute-start(f32[16,512]{1,0:T(8,128)S(1)} %fusion), channel_id=1, source_target_pairs={{0,6},{1,7},{2,8},{3,9},{4,10},{5,11},{6,12},{7,13},{8,14},{9,15},... | collective-permute-start | bytes 98312
  940.9 19.7 %collective-permute-start.4 = (f32[16,512]{1,0:T(8,128)S(1)}, f32[16,512]{1,0:T(8,128)S(1)}, u32[]{:S(2)}, u32[]{:S(2)}) collective-permute-start(f32[16,512]{1,0:T(8,128)S(1)} %fusion), channel_id=1, source_target_pairs={{0,5},{1,6},{2,7},{3,8},{4,9},{5,10},{6,11},{7,12},{8,13},{9,14},{... | collective-permute-start | bytes 98312
  (18 other events, 286.8 us)
Sparse Core Ops, SparseCore 0:
  9.8 58.0 all-gather.1
  689.9 342.3 all-reduce.23
